TPU v7x, 256 devices: a whole 4x4x8 slice. The times are simulated.
256 devices in a mesh: feat: 8 (over x, core), rows: 32 (over y, z).
Axes of the slice: x: 4, y: 4, z: 8, core: 2. Of those that a mesh axis runs over, the one named last changes fastest.
Arguments:
- kernel: float32 [8192, 8192], P('rows', 'feat'), may hold values from -0.06629126 to 5, as said below
- train_feats: float32 [16384, 8192], P('rows', 'feat'), may hold values from -6 to 6
- test_feats: float32 [8192, 8192], P('rows', 'feat'), may hold values from -6 to 6
Outputs:
- factor_state: float32 [8192, 8192], P('rows', 'feat')
- train_state: float32 [16384, 8192], P('rows', 'feat')
- test_state: float32 [8192, 8192], P('rows', 'feat')
- scores: float32 [16384, 8192], P('rows', 'feat')
Inputs may be any that keep to these rules, and one draw needn't show every extreme that they name: kernel is symmetric and positive definite; its diagonal dominates each row's other entries.
All inputs are finite; a program needn't handle non-finite values.
Results may differ from a plain program's by a relative error of at most 0.0001.
Values sent between devices are 32-bit elements; how exact they have to be, the bound alone decides.
No kernel may reach another device: no remote copies, remote signals or barrier semaphores. Data moves between devices by JAX's collectives and lax.ppermute only.
A program may use at most 128 MiB of HBM per device.

v0:
```python
import jax
import jax.numpy as jnp
from jax import lax
from jax.sharding import PartitionSpec as P

PANEL = 256
NPAN = 2


def from_root(block, axis, holder):
    block = jnp.where(lax.axis_index(axis) == holder, block, jnp.zeros_like(block))
    return lax.psum(block, axis)


def product(left, right):
    return jnp.dot(left, right, precision=lax.Precision.HIGHEST, preferred_element_type=jnp.float32)


def update_state(state, coords, right_rows):
    return state - product(coords, right_rows.T)


def per_device(kernel, train_feats, test_feats):
    blk_rows, blk_cols = kernel.shape
    row_index = lax.axis_index("rows")
    feat_index = lax.axis_index("feat")
    row_ids = row_index * blk_rows + jnp.arange(blk_rows, dtype=jnp.int32)
    col_ids = feat_index * blk_cols + jnp.arange(blk_cols, dtype=jnp.int32)
    on_panel = feat_index == 0
    identity = jnp.eye(PANEL, dtype=jnp.float32)
    matrix, train_work, test_work = (kernel, train_feats, test_feats)
    train_parts = []
    test_parts = []
    pending = None
    for panel in range(NPAN):
        first_col = panel * PANEL
        last_col = first_col + PANEL
        root_row = first_col // blk_rows
        pending = (
            matrix[:, first_col:last_col],
            matrix,
            train_work[:, first_col:last_col],
            test_work[:, first_col:last_col],
        )
        col_block, row_block, train_block, test_block = pending
        diagonal = from_root(col_block, ("feat", "rows"), root_row)
        factor = jnp.linalg.cholesky(diagonal)
        transposed = jax.scipy.linalg.solve_triangular(factor, identity, lower=True).T
        left_rows = jnp.where((row_ids >= first_col)[:, None], product(col_block, transposed), 0.0)
        train_coords = product(train_block, transposed)
        test_coords = product(test_block, transposed)
        left_rows, train_coords, test_coords = (
            from_root(left_rows, "feat", 0),
            from_root(train_coords, "feat", 0),
            from_root(test_coords, "feat", 0),
        )
        right_rows = jnp.where(
            (col_ids >= first_col)[:, None], product(row_block.T, transposed), 0.0
        )
        right_rows = from_root(right_rows, "rows", root_row)
        train_parts.append(train_coords)
        test_parts.append(test_coords)
        pending = None
        matrix = update_state(matrix, left_rows, right_rows)
        matrix = matrix.at[:, first_col:last_col].set(
            jnp.where(on_panel, left_rows, matrix[:, first_col:last_col])
        )
        train_work = update_state(train_work, train_coords, right_rows)
        train_work = train_work.at[:, first_col:last_col].set(
            jnp.where(on_panel, train_coords, train_work[:, first_col:last_col])
        )
        test_work = update_state(test_work, test_coords, right_rows)
        test_work = test_work.at[:, first_col:last_col].set(
            jnp.where(on_panel, test_coords, test_work[:, first_col:last_col])
        )
    coord_span = NPAN * PANEL
    upper = (row_ids[:, None] < coord_span) & (col_ids[None, :] >= coord_span)
    matrix = jnp.where(upper, 0.0, matrix)
    train_all = jnp.concatenate(train_parts, axis=1)
    test_all = jnp.concatenate(test_parts, axis=1)
    groups = lax.axis_size("rows") // lax.axis_size("feat")
    every_test = lax.all_gather(test_all, "rows", axis=0, tiled=True)
    wanted = lax.dynamic_slice_in_dim(
        every_test, feat_index * (groups * test_all.shape[0]), groups * test_all.shape[0], 0
    )
    scores = product(train_all, wanted.T)
    return (matrix, train_work, test_work, scores)


def solution(mesh):
    return jax.shard_map(
        per_device,
        mesh=mesh,
        in_specs=(P("rows", "feat"), P("rows", "feat"), P("rows", "feat")),
        out_specs=(P("rows", "feat"), P("rows", "feat"), P("rows", "feat"), P("rows", "feat")),
        check_vma=False,
    )
```

profile of v0, /device:TPU:2, one launch (start us, length us, event | category | flops | bytes accessed | tf_op | source)
XLA Modules:
  0.0 1282.0 jit_solution(15849999229756976496)
XLA Ops:
  7.2 1.6 copy.13
  9.6 261.8 %all-reduce.10.cloned.1.call-done = f32[256,256]{0,1:T(8,128)} async-done(((f32[256,256]{0,1:T(8,128)}), f32[256,256]{0,1:T(8,128)}) %all-reduce.10.cloned.1.call-update) | async-done | bytes 262160 | tf_op jit(solution)/shard_map/psum | solution.py:12
  273.6 11.7 cholesky.130
  285.3 9.8 custom-call.13
  295.6 11.7 cholesky.147
  309.4 4.5 while.10
  310.6 1.4 bitcast_dynamic-update-slice_fusion.4
  312.6 1.4 bitcast_dynamic-update-slice_fusion.4
  314.0 19.7 %custom-call.14 = f32[2,128,128]{1,2,0:T(8,128)S(1)} custom-call(f32[2,128,128]{2,1,0:T(8,128)S(1)} %get-tuple-element.92), custom_call_target="InvertDiagBlocksLowerTriangular" | custom-call | tf_op jit(solution)/shard_map/jit(_solve_triangular)/triangular_solve | solution.py:48
  335.7 1.4 fusion.6
  337.9 2.5 fusion.5
  340.4 2.8 fusion.4
  343.4 2.5 copy.24
  345.9 2.9 copy.18
  349.4 55.5 %all-reduce.20.cloned.1.call-done = (f32[256,256]{0,1:T(8,128)}, f32[512,256]{0,1:T(8,128)}, f32[256,256]{0,1:T(8,128)}) async-done(((f32[256,256]{0,1:T(8,128)}, f32[512,256]{0,1:T(8,128)}, f32[256,256]{0,1:T(8,128)}), (f32[256,256]{0,1:T(8,128)}, f32[512,256]{0,1:T(8,128)}, f32[256,256]{0,1:T(8,128)})) %all-reduce.20.cloned.1.call-update) | async-done | bytes 1048592 | tf_op jit(solution)/shard_map/psum | solution.py:12
  404.9 156.3 %all-reduce.12.cloned.1.call-done = f32[1024,256]{1,0:T(8,128)} async-done(((f32[1024,256]{1,0:T(8,128)}), f32[1024,256]{1,0:T(8,128)}) %all-reduce.12.cloned.1.call-update) | async-done | bytes 1048592 | tf_op jit(solution)/shard_map/psum | solution.py:12
  561.2 2.3 convolution_subtract_fusion.5
  565.2 4.0 convolution_subtract_fusion.1
  570.5 2.0 convolution_subtract_fusion.3
  572.4 2.2 fusion.19
  574.7 244.1 %all-reduce.14.cloned.1.call-done = f32[256,256]{0,1:T(8,128)} async-done(((f32[256,256]{0,1:T(8,128)}), f32[256,256]{0,1:T(8,128)}) %all-reduce.14.cloned.1.call-update) | async-done | bytes 262160 | tf_op jit(solution)/shard_map/psum | solution.py:12
  818.8 1.8 copy.15
  822.3 11.7 cholesky.164
  834.8 10.4 custom-call.15
  846.0 1.7 constant_dynamic-update-slice_fusion
  848.8 11.9 cholesky.181
  863.3 1.7 select_select_fusion.6
  865.0 5.8 while.11
  865.6 2.3 bitcast_dynamic-update-slice_fusion.5
  868.5 2.2 bitcast_dynamic-update-slice_fusion.5
  870.8 20.3 %custom-call.16 = f32[2,128,128]{1,2,0:T(8,128)} custom-call(f32[2,128,128]{2,1,0:T(8,128)S(1)} %get-tuple-element.93), custom_call_target="InvertDiagBlocksLowerTriangular" | custom-call | tf_op jit(solution)/shard_map/jit(_solve_triangular)/triangular_solve | solution.py:48
  893.3 1.2 fusion.33
  895.6 2.1 convolution_select_fusion.4
  897.7 1.4 convolution_select_fusion.2
  899.2 2.0 fusion.2
  901.5 62.1 %all-reduce.18.cloned.1.call-done = (f32[256,256]{0,1:T(8,128)}, f32[512,256]{0,1:T(8,128)}, f32[256,256]{0,1:T(8,128)}) async-done(((f32[256,256]{0,1:T(8,128)}, f32[512,256]{0,1:T(8,128)}, f32[256,256]{0,1:T(8,128)}), (f32[256,256]{0,1:T(8,128)}, f32[512,256]{0,1:T(8,128)}, f32[256,256]{0,1:T(8,128)})) %all-reduce.18.cloned.1.call-update) | async-done | bytes 1048592 | tf_op jit(solution)/shard_map/psum | solution.py:12
  963.6 1.9 pad_maximum_fusion
  966.2 153.6 %all-reduce.16.cloned.1.call-done = f32[1024,256]{1,0:T(8,128)} async-done(((f32[1024,256]{1,0:T(8,128)}), f32[1024,256]{1,0:T(8,128)}) %all-reduce.16.cloned.1.call-update) | async-done | bytes 1048592 | tf_op jit(solution)/shard_map/psum | solution.py:12
  1119.8 2.3 convolution_subtract_fusion.4
  1122.8 1.2 and_select_fusion
  1124.0 2.5 copy.28
  1126.5 4.3 convolution_subtract_fusion
  1130.8 2.5 fusion.14
  1133.3 3.0 copy.29
  1136.3 2.2 convolution_subtract_fusion.2
  1139.3 1.3 copy.30
  1140.6 127.8 %all-gather.2.cloned.1.call-done = f32[8192,512]{0,1:T(8,128)} async-done(((f32[256,512]{0,1:T(8,128)}), f32[8192,512]{0,1:T(8,128)}) %all-gather.2.cloned.1.call-update) | async-done | bytes 16777232 | tf_op jit(solution)/shard_map/all_gather | solution.py:82
  1268.4 6.4 fusion
  (93 shorter events, 24.3 us)
Async XLA Ops:
  7.2 264.3 %all-reduce.10.cloned.1.call-start = ((), (), s32[]{:S(2)}) async-start(), calls=%async_computation | async-start | bytes 524288 | tf_op jit(solution)/shard_map/psum | solution.py:12
  9.5 395.3 %all-reduce.20.cloned.1.call-start = ((), (), s32[]{:S(2)}) async-start(), calls=%async_computation.6 | async-start | bytes 2097152 | tf_op jit(solution)/shard_map/psum | solution.py:12
  334.6 5.9 copy-start.6
  340.3 220.9 %all-reduce.12.cloned.1.call-start = ((), (), s32[]{:S(2)}) async-start(), calls=%async_computation.1 | async-start | bytes 2097152 | tf_op jit(solution)/shard_map/psum | solution.py:12
  343.3 475.5 %all-reduce.14.cloned.1.call-start = ((), (), s32[]{:S(2)}) async-start(), calls=%async_computation.2 | async-start | bytes 524288 | tf_op jit(solution)/shard_map/psum | solution.py:12
  404.9 158.7 %copy-start.11 = (f32[256,256]{0,1:T(8,128)S(1)}, f32[256,256]{0,1:T(8,128)}, u32[]{:S(2)}) copy-start(f32[256,256]{0,1:T(8,128)} %get-tuple-element.117) | copy-start | bytes 786436
  564.9 398.7 %all-reduce.18.cloned.1.call-start = ((), (), s32[]{:S(2)}) async-start(), calls=%async_computation.5 | async-start | bytes 2097152 | tf_op jit(solution)/shard_map/psum | solution.py:12
  565.1 4.1 copy-start.2
  565.1 4.9 copy-start.7
  565.2 4.9 copy-start.8
  569.2 1.2 copy-start.1
  821.6 0.7 copy-start.12
  899.1 220.7 %all-reduce.16.cloned.1.call-start = ((), (), s32[]{:S(2)}) async-start(), calls=%async_computation.3 | async-start | bytes 2097152 | tf_op jit(solution)/shard_map/psum | solution.py:12
  901.2 367.2 %all-gather.2.cloned.1.call-start = ((), (), s32[]{:S(2)}) async-start(), calls=%async_computation.4 | async-start | bytes 17301504 | tf_op jit(solution)/shard_map/all_gather | solution.py:82
  965.5 156.6 %copy-start.10 = (f32[256,256]{0,1:T(8,128)S(1)}, f32[256,256]{0,1:T(8,128)}, u32[]{:S(2)}) copy-start(f32[256,256]{0,1:T(8,128)} %get-tuple-element.114) | copy-start | bytes 786436
  1122.8 3.7 copy-start
  1126.5 4.3 copy-start.4
  1133.3 3.0 copy-start.9
  1138.5 129.8 %copy-start.3 = (f32[512,256]{0,1:T(8,128)S(1)}, f32[512,256]{0,1:T(8,128)}, u32[]{:S(2)}) copy-start(f32[512,256]{0,1:T(8,128)} %get-tuple-element.118) | copy-start | bytes 1572868
  1138.5 129.8 %copy-start.5 = (f32[512,256]{0,1:T(8,128)S(1)}, f32[512,256]{0,1:T(8,128)}, u32[]{:S(2)}) copy-start(f32[512,256]{0,1:T(8,128)} %get-tuple-element.115) | copy-start | bytes 1572868
Sparse Core Ops, SparseCore 0:
  14.0 257.4 all-reduce.9
  340.5 64.3 all-reduce.19
  408.9 152.2 all-reduce.11
  567.1 251.6 all-reduce.13
  899.2 64.3 all-reduce.17
  967.5 152.2 all-reduce.15
  1122.3 146.0 all-gather.1
where the time goes:
time: 1290 us; the launch traced here: 1280 us
  waiting for transfers between devices  1060 us (82%)
  other arithmetic  127 us (10%)
  matrix products  45.5 us (4%)
  local copies, waits for them, and re-layouts  29.1 us (2%)
  between operations  17.6 us (1%)
    psum x6, waiting for transfers between devices, from_root(): return lax.psum(block, axis)  933 us
    all_gather x1, waiting for transfers between devices, per_device(): every_test = lax.all_gather(test_all, 'rows', axis=0, tiled=True)  128 us
    another operation x13, other arithmetic, per_device(): factor = jnp.linalg.cholesky(diagonal)  70 us
    another operation x5, other arithmetic, per_device(): jax.scipy.linalg.solve_triangular(factor, identity, lower=True)  41.7 us
    dot_general x15, matrix products, product(): jnp.dot(left, right, precision=lax.Precision.HIGHEST, preferred_element_t...  38 us
  transfers between devices with their start and end apart: 7, of which 7 were waited for; matrix products, arithmetic and copies ran while one was open for 3% of the time, Pallas kernels for 0%

commit v1 on v0

--- a/solution.py
+++ b/solution.py
@@ -2,9 +2,19 @@
 import jax.numpy as jnp
 from jax import lax
 from jax.sharding import PartitionSpec as P
+from jax.lax import all_to_all, axis_size
 
 PANEL = 256
 NPAN = 2
+arrange_skins = lambda a0, axis_name: jnp.concatenate(
+    all_to_all(
+        jnp.stack([a0 for _ in range(axis_size(axis_name))], axis=0),
+        axis_name=axis_name,
+        split_axis=0,
+        concat_axis=0,
+    ),
+    0,
+)
 
 
 def from_root(block, axis, holder):
@@ -79,7 +89,7 @@
     train_all = jnp.concatenate(train_parts, axis=1)
     test_all = jnp.concatenate(test_parts, axis=1)
     groups = lax.axis_size("rows") // lax.axis_size("feat")
-    every_test = lax.all_gather(test_all, "rows", axis=0, tiled=True)
+    every_test = arrange_skins(test_all, "rows")
     wanted = lax.dynamic_slice_in_dim(
         every_test, feat_index * (groups * test_all.shape[0]), groups * test_all.shape[0], 0
     )

time: 1290 us -> 1440 us (1.12)
  the two profiles are of different devices: /device:TPU:2 before, /device:TPU:15 now
where the time goes in v1:
time: 1440 us; the launch traced here: 1430 us
  waiting for transfers between devices  1190 us (83%)
  other arithmetic  128 us (9%)
  matrix products  48.7 us (3%)
  local copies, waits for them, and re-layouts  39.9 us (3%)
  between operations  17.3 us (1%)
    psum x6, waiting for transfers between devices, from_root(): return lax.psum(block, axis)  1100 us
    all_to_all x1, waiting for transfers between devices, all_to_all(jnp.stack([a0 for _ in range(axis_size(axis_name))], axis=0),...  90.7 us
    another operation x13, other arithmetic, per_device(): factor = jnp.linalg.cholesky(diagonal)  70.2 us
    another operation x5, other arithmetic, per_device(): jax.scipy.linalg.solve_triangular(factor, identity, lower=True)  41.7 us
    dot_general x15, matrix products, product(): jnp.dot(left, right, precision=lax.Precision.HIGHEST, preferred_element_t...  41.1 us
  transfers between devices with their start and end apart: 7, of which 7 were waited for; matrix products, arithmetic and copies ran while one was open for 3% of the time, Pallas kernels for 0%

profile of v1, /device:TPU:15, one launch (start us, length us, event | category | flops | bytes accessed | tf_op | source)
XLA Modules:
  0.0 1432.4 jit_solution(5135429283169273853)
XLA Ops:
  7.2 1.6 copy.13
  9.6 260.0 %all-reduce.10.cloned.1.call-done = f32[256,256]{0,1:T(8,128)} async-done(((f32[256,256]{0,1:T(8,128)}), f32[256,256]{0,1:T(8,128)}) %all-reduce.10.cloned.1.call-update) | async-done | bytes 262160 | tf_op jit(solution)/shard_map/psum | solution.py:22
  271.7 11.7 cholesky.130
  283.5 9.8 custom-call.13
  293.8 11.7 cholesky.147
  307.6 4.2 while.10
  308.4 1.4 bitcast_dynamic-update-slice_fusion.4
  310.4 1.4 bitcast_dynamic-update-slice_fusion.4
  311.8 19.7 %custom-call.14 = f32[2,128,128]{1,2,0:T(8,128)S(1)} custom-call(f32[2,128,128]{2,1,0:T(8,128)S(1)} %get-tuple-element.92), custom_call_target="InvertDiagBlocksLowerTriangular" | custom-call | tf_op jit(solution)/shard_map/jit(_solve_triangular)/triangular_solve | solution.py:58
  333.5 1.4 fusion.6
  335.7 2.5 fusion.5
  338.3 2.8 fusion.4
  341.2 2.5 copy.24
  343.7 2.9 copy.18
  347.3 58.3 %all-reduce.20.cloned.1.call-done = (f32[256,256]{0,1:T(8,128)}, f32[512,256]{0,1:T(8,128)}, f32[256,256]{0,1:T(8,128)}) async-done(((f32[256,256]{0,1:T(8,128)}, f32[512,256]{0,1:T(8,128)}, f32[256,256]{0,1:T(8,128)}), (f32[256,256]{0,1:T(8,128)}, f32[512,256]{0,1:T(8,128)}, f32[256,256]{0,1:T(8,128)})) %all-reduce.20.cloned.1.call-update) | async-done | bytes 1048592 | tf_op jit(solution)/shard_map/psum | solution.py:22
  405.6 149.1 %all-reduce.12.cloned.1.call-done = f32[1024,256]{1,0:T(8,128)} async-done(((f32[1024,256]{1,0:T(8,128)}), f32[1024,256]{1,0:T(8,128)}) %all-reduce.12.cloned.1.call-update) | async-done | bytes 1048592 | tf_op jit(solution)/shard_map/psum | solution.py:22
  554.7 2.3 convolution_subtract_fusion.5
  558.8 4.0 convolution_subtract_fusion.1
  564.1 2.0 convolution_subtract_fusion.3
  566.0 2.3 fusion.19
  568.3 248.2 %all-reduce.14.cloned.1.call-done = f32[256,256]{0,1:T(8,128)} async-done(((f32[256,256]{0,1:T(8,128)}), f32[256,256]{0,1:T(8,128)}) %all-reduce.14.cloned.1.call-update) | async-done | bytes 262160 | tf_op jit(solution)/shard_map/psum | solution.py:22
  816.6 1.8 copy.15
  820.1 11.7 cholesky.164
  832.5 10.4 custom-call.15
  843.7 1.7 constant_dynamic-update-slice_fusion
  846.5 12.1 cholesky.181
  861.2 1.7 select_select_fusion.6
  862.9 5.8 while.11
  863.5 2.3 bitcast_dynamic-update-slice_fusion.5
  866.4 2.2 bitcast_dynamic-update-slice_fusion.5
  868.6 20.3 %custom-call.16 = f32[2,128,128]{1,2,0:T(8,128)} custom-call(f32[2,128,128]{2,1,0:T(8,128)S(1)} %get-tuple-element.93), custom_call_target="InvertDiagBlocksLowerTriangular" | custom-call | tf_op jit(solution)/shard_map/jit(_solve_triangular)/triangular_solve | solution.py:58
  893.5 2.0 convolution_select_fusion.4
  895.5 1.4 convolution_select_fusion.2
  897.0 67.4 %all-reduce.18.cloned.1.call-done = (f32[256,256]{0,1:T(8,128)}, f32[512,256]{0,1:T(8,128)}, f32[256,256]{0,1:T(8,128)}) async-done(((f32[256,256]{0,1:T(8,128)}, f32[512,256]{0,1:T(8,128)}, f32[256,256]{0,1:T(8,128)}), (f32[256,256]{0,1:T(8,128)}, f32[512,256]{0,1:T(8,128)}, f32[256,256]{0,1:T(8,128)})) %all-reduce.18.cloned.1.call-update) | async-done | bytes 1048592 | tf_op jit(solution)/shard_map/psum | solution.py:22
  964.4 1.9 pad_maximum_fusion
  966.2 2.0 copy.28
  968.3 8.9 stack.2
  977.2 9.7 all-to-all-start
  986.9 2.0 fusion.2
  989.8 314.3 %all-reduce.16.cloned.1.call-done = f32[1024,256]{1,0:T(8,128)} async-done(((f32[1024,256]{1,0:T(8,128)}), f32[1024,256]{1,0:T(8,128)}) %all-reduce.16.cloned.1.call-update) | async-done | bytes 1048592 | tf_op jit(solution)/shard_map/psum | solution.py:22
  1304.1 2.3 convolution_subtract_fusion.4
  1308.3 2.5 copy.29
  1310.9 4.3 convolution_subtract_fusion
  1315.2 2.6 fusion.14
  1317.7 2.9 copy.30
  1320.7 2.2 convolution_subtract_fusion.2
  1325.0 90.7 %all-to-all-done = f32[32,256,512]{2,1,0:T(8,128)} async-done(((f32[32,256,512]{2,1,0:T(8,128)}), f32[32,256,512]{2,1,0:T(8,128)}, u32[]{:S(2)}, u32[]{:S(2)}) %all-to-all-start) | async-done | bytes 16777248 | tf_op jit(solution)/shard_map/all_to_all | solution.py:10
  1415.8 9.6 fusion
  (94 shorter events, 28.1 us)
Async XLA Ops:
  7.2 262.5 %all-reduce.10.cloned.1.call-start = ((), (), s32[]{:S(2)}) async-start(), calls=%async_computation.1 | async-start | bytes 524288 | tf_op jit(solution)/shard_map/psum | solution.py:22
  9.5 396.1 %all-reduce.20.cloned.1.call-start = ((), (), s32[]{:S(2)}) async-start(), calls=%async_computation.6 | async-start | bytes 2097152 | tf_op jit(solution)/shard_map/psum | solution.py:22
  332.4 5.9 copy-start.6
  338.2 216.5 %all-reduce.12.cloned.1.call-start = ((), (), s32[]{:S(2)}) async-start(), calls=%async_computation.2 | async-start | bytes 2097152 | tf_op jit(solution)/shard_map/psum | solution.py:22
  341.1 475.4 %all-reduce.14.cloned.1.call-start = ((), (), s32[]{:S(2)}) async-start(), calls=%async_computation.3 | async-start | bytes 524288 | tf_op jit(solution)/shard_map/psum | solution.py:22
  405.6 151.4 %copy-start.11 = (f32[256,256]{0,1:T(8,128)S(1)}, f32[256,256]{0,1:T(8,128)}, u32[]{:S(2)}) copy-start(f32[256,256]{0,1:T(8,128)} %get-tuple-element.117) | copy-start | bytes 786436
  558.5 405.9 %all-reduce.18.cloned.1.call-start = ((), (), s32[]{:S(2)}) async-start(), calls=%async_computation.5 | async-start | bytes 2097152 | tf_op jit(solution)/shard_map/psum | solution.py:22
  558.7 4.1 copy-start.2
  558.7 5.0 copy-start.7
  558.7 5.0 copy-start.8
  562.8 1.2 copy-start
  819.4 0.7 copy-start.12
  977.2 438.6 %all-to-all-start = ((f32[32,256,512]{2,1,0:T(8,128)}), f32[32,256,512]{2,1,0:T(8,128)}, u32[]{:S(2)}, u32[]{:S(2)}) async-start(f32[32,256,512]{2,1,0:T(8,128)} %stack.2), calls=%async_computation | async-start | bytes 33554432 | tf_op jit(solution)/shard_map/all_to_all | solution.py:10
  986.9 317.2 %all-reduce.16.cloned.1.call-start = ((), (), s32[]{:S(2)}) async-start(), calls=%async_computation.4 | async-start | bytes 2097152 | tf_op jit(solution)/shard_map/psum | solution.py:22
  988.9 317.5 %copy-start.10 = (f32[256,256]{0,1:T(8,128)S(1)}, f32[256,256]{0,1:T(8,128)}, u32[]{:S(2)}) copy-start(f32[256,256]{0,1:T(8,128)} %get-tuple-element.114) | copy-start | bytes 786436
  1307.1 3.7 copy-start.1
  1310.9 4.3 copy-start.4
  1317.7 2.9 copy-start.9
  1322.9 92.9 %copy-start.3 = (f32[512,256]{0,1:T(8,128)S(1)}, f32[512,256]{0,1:T(8,128)}, u32[]{:S(2)}) copy-start(f32[512,256]{0,1:T(8,128)} %get-tuple-element.118) | copy-start | bytes 1572868
  1322.9 92.9 %copy-start.5 = (f32[512,256]{0,1:T(8,128)S(1)}, f32[512,256]{0,1:T(8,128)}, u32[]{:S(2)}) copy-start(f32[512,256]{0,1:T(8,128)} %get-tuple-element.115) | copy-start | bytes 1572868
Sparse Core Ops, SparseCore 0:
  14.0 255.5 all-reduce.9
  338.3 67.2 all-reduce.19
  409.6 145.0 all-reduce.11
  560.6 255.9 all-reduce.13
  897.1 67.2 all-reduce.17
  991.4 312.6 all-reduce.15
